TPU v7x, 256 devices: a whole 4x4x8 slice. The times are simulated.
256 devices in a mesh: row: 16 (over x_lo, z), col: 16 (over x_hi, y, core).
Axes of the slice: x: 4 (x_hi: 2, x_lo: 2; x = x_hi * 2 + x_lo), y: 4, z: 8, core: 2. Of those that a mesh axis runs over, the one named last changes fastest.
Arguments:
- sp2_branch: int32 [3], replicated, may hold values from 0 to 1, as said below
- p0_occupancy: int32 [32, 32], replicated, may hold values from 0 to 1, as said below
- p1_occupancy: int32 [32, 32], replicated, may hold values from 0 to 1, as said below
- p0_columns: bfloat16 [73728, 512], P('col'), as said below
- p1_tiles: bfloat16 [3, 8192, 8192], P(None, 'row', 'col'), may hold values from -6 to 6, as said below
Outputs:
- p1_next: bfloat16 [3, 8192, 8192], P(None, 'row', 'col')
Inputs may be any that keep to these rules, and one draw needn't show every extreme that they name: `sp2_branch`: both values occur among the displacements. `p0_occupancy`: symmetric; every diagonal block is 1; blocks more than 8 apart around the circle of 32 blocks are 0. `p1_occupancy`: symmetric. `p0_columns`: the strips describe one symmetric matrix: a stored entry at row u and column v equals the stored entry at row v and column u; blocks more than 8 apart around the circle are zero. `p1_tiles`: each displacement's matrix is symmetric.
All inputs are finite; a program needn't handle non-finite values.
Results may differ from a plain program's by a relative error of at most 0.001.
Values may be sent and summed in bfloat16 or wider, within the bound.
No kernel may reach another device: no remote copies, remote signals or barrier semaphores. Data moves between devices by JAX's collectives and lax.ppermute only.
A program may use at most 192 MiB of HBM per device.

v0:
```python
import jax
import jax.numpy as jnp
from jax import lax
from jax.sharding import PartitionSpec as P

BLK = 256


def mask_blocks(values, occupancy):
    leading = values.shape[:-2]
    row_blocks = values.shape[-2] // BLK
    col_blocks = values.shape[-1] // BLK
    shaped = values.reshape(leading + (row_blocks, BLK, col_blocks, BLK))
    weight = occupancy.astype(values.dtype)[:, None, :, None]
    return (shaped * weight).reshape(values.shape)


def body(sp2_branch, p0_occupancy, p1_occupancy, p0_columns, p1_tiles):
    col_count = lax.axis_size("col")
    row_count = lax.axis_size("row")
    col_width = p0_columns.shape[1]
    row_height = p1_tiles.shape[1]
    col_blocks = col_width // BLK
    row_blocks = row_height // BLK
    strip_blocks = p0_columns.shape[0] // BLK
    band_half = (strip_blocks - col_blocks) // 2
    all_blocks = col_blocks * col_count
    col_span = band_half // col_blocks
    row_at = lax.axis_index("row")
    col_at = lax.axis_index("col")
    own_occ = lax.dynamic_slice(
        p1_occupancy, (row_at * row_blocks, col_at * col_blocks), (row_blocks, col_blocks)
    )
    p1_local = mask_blocks(p1_tiles, own_occ)
    tripled = jnp.concatenate([p0_occupancy, p0_occupancy, p0_occupancy], axis=0)
    strip_occ = lax.dynamic_slice(
        tripled,
        (col_at * col_blocks - band_half + all_blocks, col_at * col_blocks),
        (strip_blocks, col_blocks),
    )
    strip_local = mask_blocks(p0_columns, strip_occ)
    sign = jnp.where(col_at % 2 == 0, -1, 1)
    fetched = []
    for k in range(col_span):
        pairs = []
        for c in range(col_count):
            src = c - 1 - k if c % 2 == 0 else c + 1 + k
            pairs.append((src % col_count, c))
        fetched.append(lax.ppermute(p1_local, "col", pairs))
    swap = [(c, c ^ 1) for c in range(col_count)]
    partner_own = lax.ppermute(p1_local, "col", swap)
    partner_fetched = [lax.ppermute(fetched[j], "col", swap) for j in range(col_span - 1)]
    tiles = [(p1_local, 0)]
    tiles += [(fetched[k], sign * (k + 1)) for k in range(col_span)]
    tiles += [(partner_own, -sign)]
    tiles += [(partner_fetched[j], -sign * (j + 2)) for j in range(col_span - 1)]
    factors = []
    for _, offset in tiles:
        start = (offset + col_span) * col_width
        factors.append(lax.dynamic_slice_in_dim(strip_local, start, col_width, 0))
    summed_col = jnp.zeros(p1_local.shape, jnp.float32)
    for (tile, _), factor in zip(tiles, factors):
        summed_col = summed_col + jnp.einsum(
            "drc,ck->drk", tile, factor, preferred_element_type=jnp.float32
        )
    row_span = band_half // row_blocks
    owner_col = row_at * row_blocks // col_blocks
    mine = col_at == owner_col
    shared = lax.psum(jnp.where(mine, strip_local, jnp.zeros_like(strip_local)), "col")
    summed_row = jnp.zeros(p1_local.shape, jnp.float32)
    for e in range(-row_span, row_span + 1):
        if e == 0:
            incoming = p1_local
        else:
            incoming = lax.ppermute(
                p1_local, "row", [(r, (r - e) % row_count) for r in range(row_count)]
            )
        factor = shared[(e + row_span) * row_height : (e + row_span + 1) * row_height, :]
        summed_row = summed_row + jnp.einsum(
            "kr,dkc->drc", factor, incoming, preferred_element_type=jnp.float32
        )
    bracket = summed_col + summed_row
    squared = (sp2_branch == 1)[:, None, None]
    chosen = jnp.where(squared, bracket, 2.0 * p1_local.astype(jnp.float32) - bracket)
    return mask_blocks(chosen, own_occ).astype(jnp.bfloat16)


def solution(mesh):
    in_specs = (P(), P(), P(), P("col", None), P(None, "row", "col"))
    out_specs = P(None, "row", "col")
    return jax.shard_map(body, mesh=mesh, in_specs=in_specs, out_specs=out_specs, check_vma=False)
```

profile of v0, /device:TPU:67, one launch (start us, length us, event | category | flops | bytes accessed | tf_op | source)
XLA Modules:
  0.0 568.5 jit_solution(9399080054949832968)
XLA Ops:
  6.5 0.8 copy.24
  7.3 0.1 fusion.47
  7.4 0.1 copy.27
  7.5 2.5 mul.102
  10.0 3.1 copy.65
  13.1 8.1 %broadcast_select_fusion = (bf16[4608,512]{1,0:T(8,128)(2,1)}, bf16[4608,512]{1,0:T(8,128)(2,1)}) fusion(pred[]{:T(512)S(6)} %eq.13, bf16[4608,512]{1,0:T(8,128)(2,1)} %param.8, bf16[4608,512]{1,0:T(8,128)(2,1)} %bitcast.86), kind=kLoop, calls=%fused_computation.1 | loop fusion | flops 4718592 | bytes 18874368 | tf_op jit(solution)/shard_map/jit(_where)/select_n | solution.py:69
  21.1 0.0 all-reduce.2.cloned.1.call-update
  21.2 0.9 dynamic-slice_convert_fusion
  22.1 0.3 mul.98
  22.4 0.1 copy.64
  22.5 0.1 copy-done.1
  22.6 0.2 broadcast_multiply_fusion
  22.8 4.4 collective-permute-start.1
  27.1 0.0 collective-permute-start
  27.1 0.9 collective-permute-start.4
  28.0 2.0 collective-permute-start.3
  30.0 2.0 collective-permute-start.2
  32.0 7.7 %reshape.16 = bf16[18,256,2,256]{3,2,1,0:T(2,128)(2,1)} reshape(bf16[4608,512]{1,0:T(8,128)(2,1)} %param.8) | data formatting | bytes 9437184 | tf_op jit(solution)/shard_map/reshape | solution.py:13
  39.7 1.6 slice_multiply_fusion
  41.3 1.1 reshape.17
  42.4 0.3 mul.122
  42.7 0.0 slice-start
  42.7 0.1 copy.66
  42.8 0.0 copy-start.3
  42.8 3.8 fusion.48
  46.6 59.6 %collective-permute-done.1 = bf16[3,512,512]{2,1,0:T(8,128)(2,1)} collective-permute-done((bf16[3,512,512]{2,1,0:T(8,128)(2,1)S(1)}, bf16[3,512,512]{2,1,0:T(8,128)(2,1)}, u32[]{:S(2)}, u32[]{:S(2)}) %collective-permute-start.1) | collective-permute-done | bytes 1572896 | tf_op jit(solution)/shard_map/ppermute | solution.py:49
  106.3 1.7 collective-permute-start.6
  108.0 4.6 collective-permute-done
  112.6 0.0 collective-permute-start.5
  112.6 4.1 fusion.25
  116.7 4.1 fusion.27
  120.8 0.0 collective-permute-done.4
  120.8 5.2 collective-permute-start.8
  126.0 4.1 fusion.19
  130.1 27.0 %collective-permute-done.3 = bf16[3,512,512]{2,1,0:T(8,128)(2,1)} collective-permute-done((bf16[3,512,512]{2,1,0:T(8,128)(2,1)S(1)}, bf16[3,512,512]{2,1,0:T(8,128)(2,1)}, u32[]{:S(2)}, u32[]{:S(2)}) %collective-permute-start.3) | collective-permute-done | bytes 1572896 | tf_op jit(solution)/shard_map/ppermute | solution.py:49
  157.1 3.8 collective-permute-start.14
  160.9 4.1 fusion.21
  165.0 24.9 %collective-permute-start.13 = (bf16[3,512,512]{2,1,0:T(8,128)(2,1)S(1)}, bf16[3,512,512]{2,1,0:T(8,128)(2,1)}, u32[]{:S(2)}, u32[]{:S(2)}) collective-permute-start(bf16[3,512,512]{2,1,0:T(8,128)(2,1)S(1)} %broadcast_multiply_fusion), channel_id=1, source_target_pairs={{0,224},{16,240},{32,0},{48,16},{64,32},{80,48},{96,64},{112,80},{... | collective-permute-start | bytes 4718600 | tf_op jit(solution)/shard_map/ppermute | solution.py:75
  189.9 4.0 fusion.23
  193.9 0.0 collective-permute-done.6
  193.9 0.0 collective-permute-start.12
  194.0 2.6 fusion.15
  196.6 1.5 collective-permute-start.11
  198.0 2.6 fusion.17
  200.7 59.6 %all-reduce.2.cloned.1.call-done = bf16[4608,512]{1,0:T(8,128)(2,1)} async-done(((bf16[4608,512]{1,0:T(8,128)(2,1)}), bf16[4608,512]{1,0:T(8,128)(2,1)}) %all-reduce.2.cloned.1.call-update) | async-done | bytes 4718608 | tf_op jit(solution)/shard_map/psum | solution.py:69
  260.2 3.9 fusion.6
  264.1 3.5 collective-permute-start.10
  267.6 4.2 fusion.10
  271.8 21.1 %collective-permute-done.14 = bf16[3,512,512]{2,1,0:T(8,128)(2,1)} collective-permute-done((bf16[3,512,512]{2,1,0:T(8,128)(2,1)S(1)}, bf16[3,512,512]{2,1,0:T(8,128)(2,1)}, u32[]{:S(2)}, u32[]{:S(2)}) %collective-permute-start.14) | collective-permute-done | bytes 1572896 | tf_op jit(solution)/shard_map/ppermute | solution.py:75
  292.9 15.0 %collective-permute-start.9 = (bf16[3,512,512]{2,1,0:T(8,128)(2,1)S(1)}, bf16[3,512,512]{2,1,0:T(8,128)(2,1)S(1)}, u32[]{:S(2)}, u32[]{:S(2)}) collective-permute-start(bf16[3,512,512]{2,1,0:T(8,128)(2,1)S(1)} %broadcast_multiply_fusion), channel_id=1, source_target_pairs={{0,48},{16,64},{32,80},{48,96},{64,112},{80,128},{96,144},{112,160... | collective-permute-start | bytes 4718600 | tf_op jit(solution)/shard_map/ppermute | solution.py:75
  307.9 4.2 fusion.3
  312.1 56.1 %collective-permute-done.13 = bf16[3,512,512]{2,1,0:T(8,128)(2,1)} collective-permute-done((bf16[3,512,512]{2,1,0:T(8,128)(2,1)S(1)}, bf16[3,512,512]{2,1,0:T(8,128)(2,1)}, u32[]{:S(2)}, u32[]{:S(2)}) %collective-permute-start.13) | collective-permute-done | bytes 1572896 | tf_op jit(solution)/shard_map/ppermute | solution.py:75
  368.2 1.9 collective-permute-start.15
  370.1 4.1 fusion.4
  374.2 24.0 %collective-permute-done.12 = bf16[3,512,512]{2,1,0:T(8,128)(2,1)} collective-permute-done((bf16[3,512,512]{2,1,0:T(8,128)(2,1)S(1)}, bf16[3,512,512]{2,1,0:T(8,128)(2,1)}, u32[]{:S(2)}, u32[]{:S(2)}) %collective-permute-start.12) | collective-permute-done | bytes 1572896 | tf_op jit(solution)/shard_map/ppermute | solution.py:75
  398.2 1.6 collective-permute-start.7
  399.9 4.0 fusion.5
  403.9 4.1 fusion.7
  408.0 2.7 fusion.8
  410.8 26.2 %collective-permute-done.9 = bf16[3,512,512]{2,1,0:T(8,128)(2,1)S(1)} collective-permute-done((bf16[3,512,512]{2,1,0:T(8,128)(2,1)S(1)}, bf16[3,512,512]{2,1,0:T(8,128)(2,1)S(1)}, u32[]{:S(2)}, u32[]{:S(2)}) %collective-permute-start.9) | collective-permute-done | bytes 1572896 | tf_op jit(solution)/shard_map/ppermute | solution.py:75
  437.0 2.7 fusion.9
  439.7 97.9 %collective-permute-done.15 = bf16[3,512,512]{2,1,0:T(8,128)(2,1)S(1)} collective-permute-done((bf16[3,512,512]{2,1,0:T(8,128)(2,1)S(1)}, bf16[3,512,512]{2,1,0:T(8,128)(2,1)S(1)}, u32[]{:S(2)}, u32[]{:S(2)}) %collective-permute-start.15) | collective-permute-done | bytes 1572896 | tf_op jit(solution)/shard_map/ppermute | solution.py:75
  537.6 2.7 fusion.2
  540.2 21.4 %fusion.1 = bf16[3,512,512]{2,1,0:T(8,128)(2,1)} fusion(f32[3,512,512]{1,2,0:T(8,128)} %fusion.2, f32[3,512,512]{1,2,0:T(8,128)} %fusion.3, f32[3,512,512]{1,2,0:T(8,128)} %fusion.4, f32[3,512,512]{1,2,0:T(8,128)} %fusion.5, bf16[3,512,512]{2,1,0:T(8,128)(2,1)S(1)} %broadcast_multiply_fusion, f32[3,512,512]{1,2,0:T(8,128)} %fusion.6, ...), kind=kOutput, calls=%fused_computation.3 | convolution fusion | flops 823394304 | bytes 59768840 | tf_op jit(solution)/shard_map/drc,ck->drk/dot_general | solution.py:63
  (20 shorter events, 0.0 us)
Async XLA Ops:
  6.5 253.7 %all-reduce.2.cloned.1.call-start = ((), (), s32[]{:S(2)}) async-start(), calls=%async_computation | async-start | bytes 9437184 | tf_op jit(solution)/shard_map/psum | solution.py:69
  7.5 24.5 %copy-start.2 = (bf16[18,2]{1,0:T(8,128)(2,1)}, bf16[18,2]{1,0:T(8,128)(2,1)S(1)}, u32[]{:S(2)}) copy-start(bf16[18,2]{1,0:T(8,128)(2,1)S(1)} %copy.27) | copy-start | bytes 220
  21.1 1.4 copy-start.1
  22.8 83.5 %collective-permute-start.1 = (bf16[3,512,512]{2,1,0:T(8,128)(2,1)S(1)}, bf16[3,512,512]{2,1,0:T(8,128)(2,1)}, u32[]{:S(2)}, u32[]{:S(2)}) collective-permute-start(bf16[3,512,512]{2,1,0:T(8,128)(2,1)S(1)} %broadcast_multiply_fusion), channel_id=1, source_target_pairs={{14,0},{3,1},{0,2},{5,3},{2,4},{7,5},{4,6},{9,7},{6,8},{11,9},{8,1... | collective-permute-start | bytes 4718600 | tf_op jit(solution)/shard_map/ppermute | solution.py:49
  27.1 85.5 %collective-permute-start = (bf16[3,512,512]{2,1,0:T(8,128)(2,1)S(1)}, bf16[3,512,512]{2,1,0:T(8,128)(2,1)}, u32[]{:S(2)}, u32[]{:S(2)}) collective-permute-start(bf16[3,512,512]{2,1,0:T(8,128)(2,1)S(1)} %broadcast_multiply_fusion), channel_id=1, source_target_pairs={{15,0},{2,1},{1,2},{4,3},{3,4},{6,5},{5,6},{8,7},{7,8},{10,9},{9,1... | collective-permute-start | bytes 4718600 | tf_op jit(solution)/shard_map/ppermute | solution.py:49
  27.1 93.6 %collective-permute-start.4 = (bf16[3,512,512]{2,1,0:T(8,128)(2,1)S(1)}, bf16[3,512,512]{2,1,0:T(8,128)(2,1)}, u32[]{:S(2)}, u32[]{:S(2)}) collective-permute-start(bf16[3,512,512]{2,1,0:T(8,128)(2,1)S(1)} %broadcast_multiply_fusion), channel_id=1, source_target_pairs={{0,1},{1,0},{2,3},{3,2},{4,5},{5,4},{6,7},{7,6},{8,9},{9,8},{10,11... | collective-permute-start | bytes 4718600 | tf_op jit(solution)/shard_map/ppermute | solution.py:51
  28.0 129.1 %collective-permute-start.3 = (bf16[3,512,512]{2,1,0:T(8,128)(2,1)S(1)}, bf16[3,512,512]{2,1,0:T(8,128)(2,1)}, u32[]{:S(2)}, u32[]{:S(2)}) collective-permute-start(bf16[3,512,512]{2,1,0:T(8,128)(2,1)S(1)} %broadcast_multiply_fusion), channel_id=1, source_target_pairs={{12,0},{5,1},{14,2},{7,3},{0,4},{9,5},{2,6},{11,7},{4,8},{13,9},{6... | collective-permute-start | bytes 4718600 | tf_op jit(solution)/shard_map/ppermute | solution.py:49
  30.0 135.1 %collective-permute-start.2 = (bf16[3,512,512]{2,1,0:T(8,128)(2,1)S(1)}, bf16[3,512,512]{2,1,0:T(8,128)(2,1)}, u32[]{:S(2)}, u32[]{:S(2)}) collective-permute-start(bf16[3,512,512]{2,1,0:T(8,128)(2,1)S(1)} %broadcast_multiply_fusion), channel_id=1, source_target_pairs={{13,0},{4,1},{15,2},{6,3},{1,4},{8,5},{3,6},{10,7},{5,8},{12,9},{7... | collective-permute-start | bytes 4718600 | tf_op jit(solution)/shard_map/ppermute | solution.py:49
  32.0 7.7 %slice-start.2 = ((bf16[18,2]{1,0:T(8,128)(2,1)}), bf16[2,2]{1,0:T(2,128)(2,1)S(1)}, s32[]{:S(2)}) async-start(bf16[18,2]{1,0:T(8,128)(2,1)} %copy-done.2), calls=%async_computation.3 | async-start | bytes 1024 | tf_op jit(solution)/shard_map/dynamic_slice | solution.py:60
  42.7 74.0 %slice-start = ((s8[4718592]{0:T(1024)(128)(4,1)}), s8[524288]{0:T(1024)(128)(4,1)S(1)}, s32[]{:S(2)}) async-start(s8[4718592]{0:T(1024)(128)(4,1)} %bitcast.87), calls=%async_computation.1 | async-start | bytes 1048576
  42.8 3.8 copy-start.3
  42.8 73.9 %slice-start.1 = ((s8[4718592]{0:T(1024)(128)(4,1)}), s8[4194304]{0:T(1024)(128)(4,1)S(1)}, s32[]{:S(2)}) async-start(s8[4718592]{0:T(1024)(128)(4,1)} %bitcast.87), calls=%async_computation.2 | async-start | bytes 8388608
  106.3 87.7 %collective-permute-start.6 = (bf16[3,512,512]{2,1,0:T(8,128)(2,1)}, bf16[3,512,512]{2,1,0:T(8,128)(2,1)S(1)}, u32[]{:S(2)}, u32[]{:S(2)}) collective-permute-start(bf16[3,512,512]{2,1,0:T(8,128)(2,1)} %collective-permute-done.1), channel_id=1, source_target_pairs={{0,1},{1,0},{2,3},{3,2},{4,5},{5,4},{6,7},{7,6},{8,9},{9,8},{10,11... | collective-permute-start | bytes 4718600 | tf_op jit(solution)/shard_map/ppermute | solution.py:52
  112.6 84.0 %collective-permute-start.5 = (bf16[3,512,512]{2,1,0:T(8,128)(2,1)}, bf16[3,512,512]{2,1,0:T(8,128)(2,1)S(1)}, u32[]{:S(2)}, u32[]{:S(2)}) collective-permute-start(bf16[3,512,512]{2,1,0:T(8,128)(2,1)} %collective-permute-done), channel_id=1, source_target_pairs={{0,1},{1,0},{2,3},{3,2},{4,5},{5,4},{6,7},{7,6},{8,9},{9,8},{10,11... | collective-permute-start | bytes 4718600 | tf_op jit(solution)/shard_map/ppermute | solution.py:52
  120.8 143.3 %collective-permute-start.8 = (bf16[3,512,512]{2,1,0:T(8,128)(2,1)S(1)}, bf16[3,512,512]{2,1,0:T(8,128)(2,1)}, u32[]{:S(2)}, u32[]{:S(2)}) collective-permute-start(bf16[3,512,512]{2,1,0:T(8,128)(2,1)S(1)} %broadcast_multiply_fusion), channel_id=1, source_target_pairs={{0,64},{16,80},{32,96},{48,112},{64,128},{80,144},{96,160},{112,17... | collective-permute-start | bytes 4718600 | tf_op jit(solution)/shard_map/ppermute | solution.py:75
  157.1 135.8 %collective-permute-start.14 = (bf16[3,512,512]{2,1,0:T(8,128)(2,1)S(1)}, bf16[3,512,512]{2,1,0:T(8,128)(2,1)}, u32[]{:S(2)}, u32[]{:S(2)}) collective-permute-start(bf16[3,512,512]{2,1,0:T(8,128)(2,1)S(1)} %broadcast_multiply_fusion), channel_id=1, source_target_pairs={{0,208},{16,224},{32,240},{48,0},{64,16},{80,32},{96,48},{112,64},... | collective-permute-start | bytes 4718600 | tf_op jit(solution)/shard_map/ppermute | solution.py:75
  165.0 203.2 %collective-permute-start.13 = (bf16[3,512,512]{2,1,0:T(8,128)(2,1)S(1)}, bf16[3,512,512]{2,1,0:T(8,128)(2,1)}, u32[]{:S(2)}, u32[]{:S(2)}) collective-permute-start(bf16[3,512,512]{2,1,0:T(8,128)(2,1)S(1)} %broadcast_multiply_fusion), channel_id=1, source_target_pairs={{0,224},{16,240},{32,0},{48,16},{64,32},{80,48},{96,64},{112,80},{... | collective-permute-start | bytes 4718600 | tf_op jit(solution)/shard_map/ppermute | solution.py:75
  193.9 204.3 %collective-permute-start.12 = (bf16[3,512,512]{2,1,0:T(8,128)(2,1)S(1)}, bf16[3,512,512]{2,1,0:T(8,128)(2,1)}, u32[]{:S(2)}, u32[]{:S(2)}) collective-permute-start(bf16[3,512,512]{2,1,0:T(8,128)(2,1)S(1)} %broadcast_multiply_fusion), channel_id=1, source_target_pairs={{0,240},{16,0},{32,16},{48,32},{64,48},{80,64},{96,80},{112,96},{1... | collective-permute-start | bytes 4718600 | tf_op jit(solution)/shard_map/ppermute | solution.py:75
  196.6 207.4 %collective-permute-start.11 = (bf16[3,512,512]{2,1,0:T(8,128)(2,1)S(1)}, bf16[3,512,512]{2,1,0:T(8,128)(2,1)}, u32[]{:S(2)}, u32[]{:S(2)}) collective-permute-start(bf16[3,512,512]{2,1,0:T(8,128)(2,1)S(1)} %broadcast_multiply_fusion), channel_id=1, source_target_pairs={{0,16},{16,32},{32,48},{48,64},{64,80},{80,96},{96,112},{112,128},... | collective-permute-start | bytes 4718600 | tf_op jit(solution)/shard_map/ppermute | solution.py:75
  260.2 7.3 %copy-start = (bf16[4608,512]{1,0:T(8,128)(2,1)S(1)}, bf16[4608,512]{1,0:T(8,128)(2,1)}, u32[]{:S(2)}) copy-start(bf16[4608,512]{1,0:T(8,128)(2,1)} %all-reduce.2.cloned.1.call-done) | copy-start | bytes 14155780
  264.1 143.9 %collective-permute-start.10 = (bf16[3,512,512]{2,1,0:T(8,128)(2,1)S(1)}, bf16[3,512,512]{2,1,0:T(8,128)(2,1)S(1)}, u32[]{:S(2)}, u32[]{:S(2)}) collective-permute-start(bf16[3,512,512]{2,1,0:T(8,128)(2,1)S(1)} %broadcast_multiply_fusion), channel_id=1, source_target_pairs={{0,32},{16,48},{32,64},{48,80},{64,96},{80,112},{96,128},{112,144}... | collective-permute-start | bytes 4718600 | tf_op jit(solution)/shard_map/ppermute | solution.py:75
  292.9 144.1 %collective-permute-start.9 = (bf16[3,512,512]{2,1,0:T(8,128)(2,1)S(1)}, bf16[3,512,512]{2,1,0:T(8,128)(2,1)S(1)}, u32[]{:S(2)}, u32[]{:S(2)}) collective-permute-start(bf16[3,512,512]{2,1,0:T(8,128)(2,1)S(1)} %broadcast_multiply_fusion), channel_id=1, source_target_pairs={{0,48},{16,64},{32,80},{48,96},{64,112},{80,128},{96,144},{112,160... | collective-permute-start | bytes 4718600 | tf_op jit(solution)/shard_map/ppermute | solution.py:75
  368.2 169.4 %collective-permute-start.15 = (bf16[3,512,512]{2,1,0:T(8,128)(2,1)S(1)}, bf16[3,512,512]{2,1,0:T(8,128)(2,1)S(1)}, u32[]{:S(2)}, u32[]{:S(2)}) collective-permute-start(bf16[3,512,512]{2,1,0:T(8,128)(2,1)S(1)} %broadcast_multiply_fusion), channel_id=1, source_target_pairs={{0,192},{16,208},{32,224},{48,240},{64,0},{80,16},{96,32},{112,48}... | collective-permute-start | bytes 4718600 | tf_op jit(solution)/shard_map/ppermute | solution.py:75
  398.2 142.0 %collective-permute-start.7 = (bf16[3,512,512]{2,1,0:T(8,128)(2,1)}, bf16[3,512,512]{2,1,0:T(8,128)(2,1)}, u32[]{:S(2)}, u32[]{:S(2)}) collective-permute-start(bf16[3,512,512]{2,1,0:T(8,128)(2,1)} %collective-permute-done.2), channel_id=1, source_target_pairs={{0,1},{1,0},{2,3},{3,2},{4,5},{5,4},{6,7},{7,6},{8,9},{9,8},{10,11... | collective-permute-start | bytes 4718600 | tf_op jit(solution)/shard_map/ppermute | solution.py:52
Sparse Core Ops, SparseCore 0:
  21.3 238.8 all-reduce.1
where the time goes:
time: 569 us; the launch traced here: 568 us
  waiting for transfers between devices  376 us (66%)
  matrix products  83.4 us (15%)
  starting transfers between devices  68.4 us (12%)
  local copies, waits for them, and re-layouts  16.2 us (3%)
  between operations  13.5 us (2%)
  other arithmetic  10.8 us (2%)
    ppermute x8, waiting for transfers between devices, body(): lax.ppermute(p1_local, 'row', [(r, (r - e) % row_count) for r in range(ro...  225 us
    ppermute x4, waiting for transfers between devices, body(): fetched.append(lax.ppermute(p1_local, 'col', pairs))  91.2 us
    psum x1, waiting for transfers between devices, body(): lax.psum(jnp.where(mine, strip_local, jnp.zeros_like(strip_local)), 'col')  59.6 us
    ppermute x8, starting transfers between devices, body(): lax.ppermute(p1_local, 'row', [(r, (r - e) % row_count) for r in range(ro...  55.8 us
    dot_general x9, matrix products, body(): jnp.einsum('drc,ck->drk', tile, factor, preferred_element_type=jnp.float32)  50.8 us
    dot_general x9, matrix products, body(): jnp.einsum('kr,dkc->drc', factor, incoming, preferred_element_type=jnp.fl...  32.6 us
  transfers between devices with their start and end apart: 17, of which 9 were waited for; matrix products, arithmetic and copies ran while one was open for 13% of the time, Pallas kernels for 0%

commit v1 on v0

--- a/solution.py
+++ b/solution.py
@@ -66,7 +66,9 @@
     row_span = band_half // row_blocks
     owner_col = row_at * row_blocks // col_blocks
     mine = col_at == owner_col
-    shared = lax.psum(jnp.where(mine, strip_local, jnp.zeros_like(strip_local)), "col")
+    block = jnp.where(mine, strip_local, jnp.zeros_like(strip_local))
+    pieces = lax.all_gather(block, "col")
+    shared = jnp.sum(pieces, axis=0)
     summed_row = jnp.zeros(p1_local.shape, jnp.float32)
     for e in range(-row_span, row_span + 1):
         if e == 0:

time: 569 us -> 878 us (1.54)
  the two profiles are of different devices: /device:TPU:67 before, /device:TPU:13 now
where the time goes in v1:
time: 878 us
  waiting for transfers between devices  585 us (67%)
  starting transfers between devices  142 us (16%)
  matrix products  83.7 us (10%)
  other arithmetic  37.4 us (4%)
  local copies, waits for them, and re-layouts  16.4 us (2%)
  between operations  13.5 us (2%)
    all_gather x1, waiting for transfers between devices, body(): pieces = lax.all_gather(block, 'col')  310 us
    ppermute x8, waiting for transfers between devices, body(): lax.ppermute(p1_local, 'row', [(r, (r - e) % row_count) for r in range(ro...  199 us
    ppermute x8, starting transfers between devices, body(): lax.ppermute(p1_local, 'row', [(r, (r - e) % row_count) for r in range(ro...  118 us
    ppermute x4, waiting for transfers between devices, body(): fetched.append(lax.ppermute(p1_local, 'col', pairs))  76 us
    dot_general x9, matrix products, body(): jnp.einsum('drc,ck->drk', tile, factor, preferred_element_type=jnp.float32)  51.2 us
    dot_general x9, matrix products, body(): jnp.einsum('kr,dkc->drc', factor, incoming, preferred_element_type=jnp.fl...  32.5 us
    reduce_sum x1, other arithmetic, body(): shared = jnp.sum(pieces, axis=0)  26.4 us
  transfers between devices with their start and end apart: 17, of which 4 were waited for; matrix products, arithmetic and copies ran while one was open for 12% of the time, Pallas kernels for 0%

profile of v1, /device:TPU:13, one launch (start us, length us, event | category | flops | bytes accessed | tf_op | source)
XLA Modules:
  0.0 877.7 jit_solution(6487829330307453895)
XLA Ops:
  6.5 0.8 copy.24
  7.3 0.1 fusion.47
  7.4 0.1 copy.27
  7.5 2.5 mul.102
  10.0 3.0 copy.65
  13.0 8.1 broadcast_select_fusion
  21.1 0.0 all-gather.3.cloned.1.call-update
  21.1 0.9 dynamic-slice_convert_fusion
  22.0 0.3 mul.98
  22.4 0.1 copy.64
  22.5 0.1 copy-done.1
  22.5 0.2 broadcast_multiply_fusion
  22.7 0.2 collective-permute-start.1
  23.0 3.0 collective-permute-start
  25.9 0.1 collective-permute-start.4
  26.1 3.3 collective-permute-start.3
  29.3 2.3 collective-permute-start.2
  31.7 7.9 reshape.16
  39.6 1.7 slice_multiply_fusion
  41.3 1.1 reshape.18
  42.4 0.3 mul.122
  42.7 0.0 slice-start
  42.8 0.1 copy.66
  42.8 0.0 copy-start.3
  42.9 0.0 slice-start.1
  42.9 4.1 fusion.48
  46.9 58.1 %collective-permute-done.1 = bf16[3,512,512]{2,1,0:T(8,128)(2,1)} collective-permute-done((bf16[3,512,512]{2,1,0:T(8,128)(2,1)S(1)}, bf16[3,512,512]{2,1,0:T(8,128)(2,1)}, u32[]{:S(2)}, u32[]{:S(2)}) %collective-permute-start.1) | collective-permute-done | bytes 1572896 | tf_op jit(solution)/shard_map/ppermute | solution.py:49
  105.0 13.7 %collective-permute-start.5 = (bf16[3,512,512]{2,1,0:T(8,128)(2,1)}, bf16[3,512,512]{2,1,0:T(8,128)(2,1)S(1)}, u32[]{:S(2)}, u32[]{:S(2)}) collective-permute-start(bf16[3,512,512]{2,1,0:T(8,128)(2,1)} %collective-permute-done), channel_id=1, source_target_pairs={{0,1},{1,0},{2,3},{3,2},{4,5},{5,4},{6,7},{7,6},{8,9},{9,8},{10,11... | collective-permute-start | bytes 4718600 | tf_op jit(solution)/shard_map/ppermute | solution.py:52
  118.7 4.2 fusion.25
  122.9 4.1 fusion.27
  127.0 0.0 collective-permute-done.4
  127.0 7.9 collective-permute-start.8
  134.8 4.2 fusion.19
  139.1 17.9 %collective-permute-done.3 = bf16[3,512,512]{2,1,0:T(8,128)(2,1)} collective-permute-done((bf16[3,512,512]{2,1,0:T(8,128)(2,1)S(1)}, bf16[3,512,512]{2,1,0:T(8,128)(2,1)}, u32[]{:S(2)}, u32[]{:S(2)}) %collective-permute-start.3) | collective-permute-done | bytes 1572896 | tf_op jit(solution)/shard_map/ppermute | solution.py:49
  157.0 20.7 %collective-permute-start.14 = (bf16[3,512,512]{2,1,0:T(8,128)(2,1)S(1)}, bf16[3,512,512]{2,1,0:T(8,128)(2,1)}, u32[]{:S(2)}, u32[]{:S(2)}) collective-permute-start(bf16[3,512,512]{2,1,0:T(8,128)(2,1)S(1)} %broadcast_multiply_fusion), channel_id=1, source_target_pairs={{0,208},{16,224},{32,240},{48,0},{64,16},{80,32},{96,48},{112,64},... | collective-permute-start | bytes 4718600 | tf_op jit(solution)/shard_map/ppermute | solution.py:77
  177.7 4.0 fusion.21
  181.7 0.3 collective-permute-start.13
  182.0 4.0 fusion.23
  186.0 0.0 collective-permute-done.6
  186.0 0.5 collective-permute-start.12
  186.5 2.6 fusion.15
  189.1 0.0 collective-permute-done.5
  189.1 1.1 collective-permute-start.11
  190.2 2.6 fusion.17
  192.9 310.1 %all-gather.3.cloned.1.call-done = bf16[73728,512]{1,0:T(8,128)(2,1)} async-done(((bf16[4608,512]{1,0:T(8,128)(2,1)}), bf16[73728,512]{1,0:T(8,128)(2,1)}) %all-gather.3.cloned.1.call-update) | async-done | bytes 75497488 | tf_op jit(solution)/shard_map/all_gather | solution.py:70
  503.0 26.4 %reduce_sum.12 = bf16[4608,512]{1,0:T(8,128)(2,1)} reduce(bf16[16,4608,512]{2,1,0:T(8,128)(2,1)} %bitcast.8, bf16[]{:T(256)} %constant.57.clone.1), dimensions={0}, to_apply=%region_0.1 | reduce | flops 35389440 | bytes 80216064 | tf_op jit(solution)/shard_map/reduce_sum | solution.py:71
  529.4 3.8 fusion.6
  533.3 0.0 collective-permute-done.8
  533.3 0.0 collective-permute-start.10
  533.3 4.1 fusion.10
  537.4 20.6 %collective-permute-start.9 = (bf16[3,512,512]{2,1,0:T(8,128)(2,1)S(1)}, bf16[3,512,512]{2,1,0:T(8,128)(2,1)S(1)}, u32[]{:S(2)}, u32[]{:S(2)}) collective-permute-start(bf16[3,512,512]{2,1,0:T(8,128)(2,1)S(1)} %broadcast_multiply_fusion), channel_id=1, source_target_pairs={{0,48},{16,64},{32,80},{48,96},{64,112},{80,128},{96,144},{112,160... | collective-permute-start | bytes 4718600 | tf_op jit(solution)/shard_map/ppermute | solution.py:77
  558.0 4.1 fusion.3
  562.1 0.0 collective-permute-done.13
  562.1 67.0 %collective-permute-start.15 = (bf16[3,512,512]{2,1,0:T(8,128)(2,1)S(1)}, bf16[3,512,512]{2,1,0:T(8,128)(2,1)S(1)}, u32[]{:S(2)}, u32[]{:S(2)}) collective-permute-start(bf16[3,512,512]{2,1,0:T(8,128)(2,1)S(1)} %broadcast_multiply_fusion), channel_id=1, source_target_pairs={{0,192},{16,208},{32,224},{48,240},{64,0},{80,16},{96,32},{112,48}... | collective-permute-start | bytes 4718600 | tf_op jit(solution)/shard_map/ppermute | solution.py:77
  629.1 4.2 fusion.4
  633.3 0.8 collective-permute-start.7
  634.1 4.1 fusion.5
  638.2 4.1 fusion.7
  642.3 0.0 collective-permute-done.10
  642.3 2.7 fusion.8
  645.1 199.0 %collective-permute-done.9 = bf16[3,512,512]{2,1,0:T(8,128)(2,1)S(1)} collective-permute-done((bf16[3,512,512]{2,1,0:T(8,128)(2,1)S(1)}, bf16[3,512,512]{2,1,0:T(8,128)(2,1)S(1)}, u32[]{:S(2)}, u32[]{:S(2)}) %collective-permute-start.9) | collective-permute-done | bytes 1572896 | tf_op jit(solution)/shard_map/ppermute | solution.py:77
  844.1 2.8 fusion.9
  846.8 2.7 fusion.2
  849.5 21.4 %fusion.1 = bf16[3,512,512]{2,1,0:T(8,128)(2,1)} fusion(f32[3,512,512]{1,2,0:T(8,128)} %fusion.2, f32[3,512,512]{1,2,0:T(8,128)} %fusion.3, f32[3,512,512]{1,2,0:T(8,128)} %fusion.4, f32[3,512,512]{1,2,0:T(8,128)} %fusion.5, bf16[3,512,512]{2,1,0:T(8,128)(2,1)S(1)} %broadcast_multiply_fusion, f32[3,512,512]{1,2,0:T(8,128)} %fusion.6, ...), kind=kOutput, calls=%fused_computation.3 | convolution fusion | flops 823394304 | bytes 59768840 | tf_op jit(solution)/shard_map/drc,ck->drk/dot_general | solution.py:63
  (21 shorter events, 0.0 us)
Async XLA Ops:
  6.5 496.5 %all-gather.3.cloned.1.call-start = ((), (), s32[]{:S(2)}) async-start(), calls=%async_computation | async-start | bytes 80216064 | tf_op jit(solution)/shard_map/all_gather | solution.py:70
  7.5 24.1 %copy-start.2 = (bf16[18,2]{1,0:T(8,128)(2,1)}, bf16[18,2]{1,0:T(8,128)(2,1)S(1)}, u32[]{:S(2)}) copy-start(bf16[18,2]{1,0:T(8,128)(2,1)S(1)} %copy.27) | copy-start | bytes 220
  21.1 1.4 copy-start.1
  22.7 82.3 %collective-permute-start.1 = (bf16[3,512,512]{2,1,0:T(8,128)(2,1)S(1)}, bf16[3,512,512]{2,1,0:T(8,128)(2,1)}, u32[]{:S(2)}, u32[]{:S(2)}) collective-permute-start(bf16[3,512,512]{2,1,0:T(8,128)(2,1)S(1)} %broadcast_multiply_fusion), channel_id=1, source_target_pairs={{14,0},{3,1},{0,2},{5,3},{2,4},{7,5},{4,6},{9,7},{6,8},{11,9},{8,1... | collective-permute-start | bytes 4718600 | tf_op jit(solution)/shard_map/ppermute | solution.py:49
  23.0 82.1 %collective-permute-start = (bf16[3,512,512]{2,1,0:T(8,128)(2,1)S(1)}, bf16[3,512,512]{2,1,0:T(8,128)(2,1)}, u32[]{:S(2)}, u32[]{:S(2)}) collective-permute-start(bf16[3,512,512]{2,1,0:T(8,128)(2,1)S(1)} %broadcast_multiply_fusion), channel_id=1, source_target_pairs={{15,0},{2,1},{1,2},{4,3},{3,4},{6,5},{5,6},{8,7},{7,8},{10,9},{9,1... | collective-permute-start | bytes 4718600 | tf_op jit(solution)/shard_map/ppermute | solution.py:49
  25.9 101.0 %collective-permute-start.4 = (bf16[3,512,512]{2,1,0:T(8,128)(2,1)S(1)}, bf16[3,512,512]{2,1,0:T(8,128)(2,1)}, u32[]{:S(2)}, u32[]{:S(2)}) collective-permute-start(bf16[3,512,512]{2,1,0:T(8,128)(2,1)S(1)} %broadcast_multiply_fusion), channel_id=1, source_target_pairs={{0,1},{1,0},{2,3},{3,2},{4,5},{5,4},{6,7},{7,6},{8,9},{9,8},{10,11... | collective-permute-start | bytes 4718600 | tf_op jit(solution)/shard_map/ppermute | solution.py:51
  26.1 130.9 %collective-permute-start.3 = (bf16[3,512,512]{2,1,0:T(8,128)(2,1)S(1)}, bf16[3,512,512]{2,1,0:T(8,128)(2,1)}, u32[]{:S(2)}, u32[]{:S(2)}) collective-permute-start(bf16[3,512,512]{2,1,0:T(8,128)(2,1)S(1)} %broadcast_multiply_fusion), channel_id=1, source_target_pairs={{12,0},{5,1},{14,2},{7,3},{0,4},{9,5},{2,6},{11,7},{4,8},{13,9},{6... | collective-permute-start | bytes 4718600 | tf_op jit(solution)/shard_map/ppermute | solution.py:49
  29.3 152.4 %collective-permute-start.2 = (bf16[3,512,512]{2,1,0:T(8,128)(2,1)S(1)}, bf16[3,512,512]{2,1,0:T(8,128)(2,1)}, u32[]{:S(2)}, u32[]{:S(2)}) collective-permute-start(bf16[3,512,512]{2,1,0:T(8,128)(2,1)S(1)} %broadcast_multiply_fusion), channel_id=1, source_target_pairs={{13,0},{4,1},{15,2},{6,3},{1,4},{8,5},{3,6},{10,7},{5,8},{12,9},{7... | collective-permute-start | bytes 4718600 | tf_op jit(solution)/shard_map/ppermute | solution.py:49
  31.7 7.9 slice-start.2
  42.7 80.1 %slice-start = ((s8[4718592]{0:T(1024)(128)(4,1)}), s8[524288]{0:T(1024)(128)(4,1)S(1)}, s32[]{:S(2)}) async-start(s8[4718592]{0:T(1024)(128)(4,1)} %bitcast.88), calls=%async_computation.1 | async-start | bytes 1048576
  42.8 4.1 copy-start.3
  42.9 80.0 %slice-start.1 = ((s8[4718592]{0:T(1024)(128)(4,1)}), s8[4194304]{0:T(1024)(128)(4,1)S(1)}, s32[]{:S(2)}) async-start(s8[4718592]{0:T(1024)(128)(4,1)} %bitcast.88), calls=%async_computation.2 | async-start | bytes 8388608
  105.0 81.0 %collective-permute-start.6 = (bf16[3,512,512]{2,1,0:T(8,128)(2,1)}, bf16[3,512,512]{2,1,0:T(8,128)(2,1)S(1)}, u32[]{:S(2)}, u32[]{:S(2)}) collective-permute-start(bf16[3,512,512]{2,1,0:T(8,128)(2,1)} %collective-permute-done.1), channel_id=1, source_target_pairs={{0,1},{1,0},{2,3},{3,2},{4,5},{5,4},{6,7},{7,6},{8,9},{9,8},{10,11... | collective-permute-start | bytes 4718600 | tf_op jit(solution)/shard_map/ppermute | solution.py:52
  105.0 84.1 %collective-permute-start.5 = (bf16[3,512,512]{2,1,0:T(8,128)(2,1)}, bf16[3,512,512]{2,1,0:T(8,128)(2,1)S(1)}, u32[]{:S(2)}, u32[]{:S(2)}) collective-permute-start(bf16[3,512,512]{2,1,0:T(8,128)(2,1)} %collective-permute-done), channel_id=1, source_target_pairs={{0,1},{1,0},{2,3},{3,2},{4,5},{5,4},{6,7},{7,6},{8,9},{9,8},{10,11... | collective-permute-start | bytes 4718600 | tf_op jit(solution)/shard_map/ppermute | solution.py:52
  127.0 406.3 %collective-permute-start.8 = (bf16[3,512,512]{2,1,0:T(8,128)(2,1)S(1)}, bf16[3,512,512]{2,1,0:T(8,128)(2,1)}, u32[]{:S(2)}, u32[]{:S(2)}) collective-permute-start(bf16[3,512,512]{2,1,0:T(8,128)(2,1)S(1)} %broadcast_multiply_fusion), channel_id=1, source_target_pairs={{0,64},{16,80},{32,96},{48,112},{64,128},{80,144},{96,160},{112,17... | collective-permute-start | bytes 4718600 | tf_op jit(solution)/shard_map/ppermute | solution.py:77
  157.0 380.4 %collective-permute-start.14 = (bf16[3,512,512]{2,1,0:T(8,128)(2,1)S(1)}, bf16[3,512,512]{2,1,0:T(8,128)(2,1)}, u32[]{:S(2)}, u32[]{:S(2)}) collective-permute-start(bf16[3,512,512]{2,1,0:T(8,128)(2,1)S(1)} %broadcast_multiply_fusion), channel_id=1, source_target_pairs={{0,208},{16,224},{32,240},{48,0},{64,16},{80,32},{96,48},{112,64},... | collective-permute-start | bytes 4718600 | tf_op jit(solution)/shard_map/ppermute | solution.py:77
  181.7 380.4 %collective-permute-start.13 = (bf16[3,512,512]{2,1,0:T(8,128)(2,1)S(1)}, bf16[3,512,512]{2,1,0:T(8,128)(2,1)}, u32[]{:S(2)}, u32[]{:S(2)}) collective-permute-start(bf16[3,512,512]{2,1,0:T(8,128)(2,1)S(1)} %broadcast_multiply_fusion), channel_id=1, source_target_pairs={{0,224},{16,240},{32,0},{48,16},{64,32},{80,48},{96,64},{112,80},{... | collective-permute-start | bytes 4718600 | tf_op jit(solution)/shard_map/ppermute | solution.py:77
  186.0 447.3 %collective-permute-start.12 = (bf16[3,512,512]{2,1,0:T(8,128)(2,1)S(1)}, bf16[3,512,512]{2,1,0:T(8,128)(2,1)}, u32[]{:S(2)}, u32[]{:S(2)}) collective-permute-start(bf16[3,512,512]{2,1,0:T(8,128)(2,1)S(1)} %broadcast_multiply_fusion), channel_id=1, source_target_pairs={{0,240},{16,0},{32,16},{48,32},{64,48},{80,64},{96,80},{112,96},{1... | collective-permute-start | bytes 4718600 | tf_op jit(solution)/shard_map/ppermute | solution.py:77
  189.1 449.1 %collective-permute-start.11 = (bf16[3,512,512]{2,1,0:T(8,128)(2,1)S(1)}, bf16[3,512,512]{2,1,0:T(8,128)(2,1)}, u32[]{:S(2)}, u32[]{:S(2)}) collective-permute-start(bf16[3,512,512]{2,1,0:T(8,128)(2,1)S(1)} %broadcast_multiply_fusion), channel_id=1, source_target_pairs={{0,16},{16,32},{32,48},{48,64},{64,80},{80,96},{96,112},{112,128},... | collective-permute-start | bytes 4718600 | tf_op jit(solution)/shard_map/ppermute | solution.py:77
  529.4 3.9 copy-start
  533.3 109.0 %collective-permute-start.10 = (bf16[3,512,512]{2,1,0:T(8,128)(2,1)S(1)}, bf16[3,512,512]{2,1,0:T(8,128)(2,1)S(1)}, u32[]{:S(2)}, u32[]{:S(2)}) collective-permute-start(bf16[3,512,512]{2,1,0:T(8,128)(2,1)S(1)} %broadcast_multiply_fusion), channel_id=1, source_target_pairs={{0,32},{16,48},{32,64},{48,80},{64,96},{80,112},{96,128},{112,144}... | collective-permute-start | bytes 4718600 | tf_op jit(solution)/shard_map/ppermute | solution.py:77
  537.4 306.7 %collective-permute-start.9 = (bf16[3,512,512]{2,1,0:T(8,128)(2,1)S(1)}, bf16[3,512,512]{2,1,0:T(8,128)(2,1)S(1)}, u32[]{:S(2)}, u32[]{:S(2)}) collective-permute-start(bf16[3,512,512]{2,1,0:T(8,128)(2,1)S(1)} %broadcast_multiply_fusion), channel_id=1, source_target_pairs={{0,48},{16,64},{32,80},{48,96},{64,112},{80,128},{96,144},{112,160... | collective-permute-start | bytes 4718600 | tf_op jit(solution)/shard_map/ppermute | solution.py:77
  562.1 284.7 %collective-permute-start.15 = (bf16[3,512,512]{2,1,0:T(8,128)(2,1)S(1)}, bf16[3,512,512]{2,1,0:T(8,128)(2,1)S(1)}, u32[]{:S(2)}, u32[]{:S(2)}) collective-permute-start(bf16[3,512,512]{2,1,0:T(8,128)(2,1)S(1)} %broadcast_multiply_fusion), channel_id=1, source_target_pairs={{0,192},{16,208},{32,224},{48,240},{64,0},{80,16},{96,32},{112,48}... | collective-permute-start | bytes 4718600 | tf_op jit(solution)/shard_map/ppermute | solution.py:77
  633.3 216.2 %collective-permute-start.7 = (bf16[3,512,512]{2,1,0:T(8,128)(2,1)}, bf16[3,512,512]{2,1,0:T(8,128)(2,1)}, u32[]{:S(2)}, u32[]{:S(2)}) collective-permute-start(bf16[3,512,512]{2,1,0:T(8,128)(2,1)} %collective-permute-done.2), channel_id=1, source_target_pairs={{0,1},{1,0},{2,3},{3,2},{4,5},{5,4},{6,7},{7,6},{8,9},{9,8},{10,11... | collective-permute-start | bytes 4718600 | tf_op jit(solution)/shard_map/ppermute | solution.py:52
Sparse Core Ops, SparseCore 0:
  21.3 481.7 all-gather.2
